TPU v7x, 256 devices: a whole 4x4x8 slice. The times are simulated.
256 devices in a mesh: seq: 32 (over z, x), dp: 8 (over y, core).
Axes of the slice: x: 4, y: 4, z: 8, core: 2. Of those that a mesh axis runs over, the one named last changes fastest.
Arguments:
- query_rows: bfloat16 [8, 4096, 2048], P('dp', 'seq'), may hold values from -6 to 6
- key_rows: bfloat16 [8, 4096, 2048], P('dp', 'seq'), may hold values from -6 to 6
- value_rows: bfloat16 [8, 4096, 2048], P('dp', 'seq'), may hold values from -6 to 6
- out_grad: bfloat16 [8, 4096, 4096], P('dp', 'seq'), may hold values from -6 to 6
- rand_blocks: int32 [8, 64, 3], P('dp'), may hold values from 0 to 63
- global_tokens: int32 [8, 128], P('dp'), may hold values from 0 to 4095, as said below
- out_proj: bfloat16 [2048, 4096], P('dp'), may hold values from -0.125 to 0.125
Outputs:
- grad_queries: bfloat16 [8, 4096, 2048], P('dp', 'seq')
- grad_keys: bfloat16 [8, 4096, 2048], P('dp', 'seq')
- grad_values: bfloat16 [8, 4096, 2048], P('dp', 'seq')
- grad_out_proj: bfloat16 [2048, 4096], P('dp')
Inputs may be any that keep to these rules, and one draw needn't show every extreme that they name: `global_tokens`: in each document window 128 distinct positions in increasing order; the first and the last position of the window are always among them.
All inputs are finite; a program needn't handle non-finite values.
Results may differ from a plain program's by a relative error of at most 0.012.
Values may be sent and summed in bfloat16 or wider, within the bound.
No kernel may reach another device: no remote copies, remote signals or barrier semaphores. Data moves between devices by JAX's collectives and lax.ppermute only.
A program may use at most 128 MiB of HBM per device.

v0:
```python
import math

import jax
import jax.numpy as jnp
from jax import lax
from jax.sharding import PartitionSpec as P

HEAD_DIM = 128
BLOCK = 64
RANDOM = 3


MASKED = -1e30


def softmax_rows(scores):
    highest = jnp.max(scores, axis=-1, keepdims=True)
    raised = jnp.exp(scores - highest)
    return raised / jnp.sum(raised, axis=-1, keepdims=True)


def shards(query_rows, key_rows, value_rows, out_grad, rand_blocks, global_tokens, out_proj):
    seq_devices = lax.axis_size("seq")
    dp_devices = lax.axis_size("dp")
    tokens = query_rows.shape[1]
    width = query_rows.shape[2]
    model_width = out_grad.shape[2]
    head_count = width // HEAD_DIM
    splitting = max(seq_devices // head_count, 1)
    heads_here = max(head_count // seq_devices, 1)
    columns = heads_here * HEAD_DIM
    head_groups = seq_devices // splitting
    slice_rows = tokens // splitting
    seq_length = tokens * seq_devices
    block_total = seq_length // BLOCK
    window_keys = (3 + RANDOM) * BLOCK
    query_count = seq_devices * slice_rows
    query_blocks = query_count // BLOCK
    owned_groups = seq_devices // dp_devices // splitting
    global_count = global_tokens.shape[1]
    scaling = 1.0 / math.sqrt(HEAD_DIM)
    my_slice = lax.axis_index("seq") % splitting
    doc_blocks = rand_blocks[0]
    doc_globals = global_tokens[0]
    query_send = (
        query_rows[0]
        .reshape(splitting, slice_rows, head_groups, columns)
        .transpose(2, 0, 1, 3)
        .reshape(seq_devices, slice_rows, columns)
    )

    def spread(rows):
        grouped = rows[0].reshape(tokens, head_groups, columns).transpose(1, 0, 2)
        return jnp.broadcast_to(
            grouped[:, None], (head_groups, splitting, tokens, columns)
        ).reshape(seq_devices, tokens, columns)

    query_head, key_head, value_head = (
        lax.all_to_all(query_send, "seq", split_axis=0, concat_axis=0, tiled=True),
        lax.all_to_all(spread(key_rows), "seq", split_axis=0, concat_axis=0, tiled=True),
        lax.all_to_all(spread(value_rows), "seq", split_axis=0, concat_axis=0, tiled=True),
    )
    source_start = jnp.arange(seq_devices, dtype=jnp.int32)[:, None] * tokens
    offsets = jnp.arange(slice_rows, dtype=jnp.int32)[None, :]
    query_pos = (source_start + my_slice * slice_rows + offsets).reshape(query_count)
    block_of = query_pos.reshape(query_blocks, BLOCK)[:, 0] // BLOCK
    window = block_of[:, None] + jnp.arange(-1, 2, dtype=jnp.int32)[None, :]
    inside = (window >= 0) & (window < block_total)
    block_ids = jnp.concatenate(
        [jnp.clip(window, 0, block_total - 1), jnp.take(doc_blocks, block_of, axis=0)], axis=1
    )
    usable = jnp.concatenate(
        [jnp.repeat(inside, BLOCK, axis=1), jnp.ones((query_blocks, RANDOM * BLOCK), dtype=bool)],
        axis=1,
    )
    key_all = key_head.reshape(seq_length, heads_here, HEAD_DIM)
    value_all = value_head.reshape(seq_length, heads_here, HEAD_DIM)
    key_win = key_all.reshape(block_total, BLOCK, heads_here, HEAD_DIM)[block_ids].reshape(
        query_blocks, window_keys, heads_here, HEAD_DIM
    )
    value_win = value_all.reshape(block_total, BLOCK, heads_here, HEAD_DIM)[block_ids].reshape(
        query_blocks, window_keys, heads_here, HEAD_DIM
    )
    key_glob = jnp.take(key_all, doc_globals, axis=0)
    value_glob = jnp.take(value_all, doc_globals, axis=0)
    query_blk = query_head.reshape(query_blocks, BLOCK, heads_here, HEAD_DIM)
    score_win = (
        jnp.einsum("bqhe,bkhe->bhqk", query_blk, key_win, preferred_element_type=jnp.float32)
        * scaling
    )
    score_win = jnp.where(usable[:, None, None, :], score_win, MASKED)
    score_glob = (
        jnp.einsum("bqhe,khe->bhqk", query_blk, key_glob, preferred_element_type=jnp.float32)
        * scaling
    )
    prob_rows = softmax_rows(jnp.concatenate([score_win, score_glob], axis=-1))
    prob_bf = prob_rows.astype(jnp.bfloat16)
    sparse_out = jnp.einsum(
        "bhqk,bkhe->bqhe", prob_bf[..., :window_keys], value_win, preferred_element_type=jnp.float32
    )
    sparse_out = sparse_out + jnp.einsum(
        "bhqk,khe->bqhe", prob_bf[..., window_keys:], value_glob, preferred_element_type=jnp.float32
    )
    matches = query_pos[:, None] == doc_globals[None, :]
    picker = matches.astype(jnp.bfloat16)
    picker_f = matches.astype(jnp.float32)
    is_global = jnp.any(matches, axis=1)
    query_glob = (
        jnp.einsum(
            "ng,nc->gc",
            picker,
            query_head.reshape(query_count, columns),
            preferred_element_type=jnp.float32,
        )
        .astype(jnp.bfloat16)
        .reshape(global_count, heads_here, HEAD_DIM)
    )
    prob_glob = softmax_rows(
        jnp.einsum("ghe,the->hgt", query_glob, key_all, preferred_element_type=jnp.float32)
        * scaling
    )
    prob_glob_bf = prob_glob.astype(jnp.bfloat16)
    glob_out = jnp.einsum(
        "hgt,the->ghe", prob_glob_bf, value_all, preferred_element_type=jnp.float32
    ).reshape(global_count, columns)
    placed = jnp.dot(picker_f, glob_out, precision=lax.Precision.HIGHEST)
    attention = jnp.where(
        is_global[:, None], placed, sparse_out.reshape(query_count, columns)
    ).astype(jnp.bfloat16)
    owned = lax.all_to_all(
        lax.all_to_all(
            attention.reshape(1, seq_devices, slice_rows, columns),
            "seq",
            split_axis=1,
            concat_axis=1,
            tiled=True,
        ),
        "dp",
        split_axis=1,
        concat_axis=0,
        tiled=True,
    )
    owned = owned.reshape(dp_devices, owned_groups, splitting, slice_rows, columns)
    proj_rows = out_proj.reshape(owned_groups, columns, model_width)
    piece_rows = lax.all_gather(out_grad, "dp", axis=0, tiled=True)
    doc_count = piece_rows.shape[0]
    grads = piece_rows.reshape(doc_count, splitting, slice_rows, model_width)
    local_delta = jnp.einsum(
        "kptd,gcd->kgptc", grads, proj_rows, preferred_element_type=jnp.float32
    ).astype(jnp.bfloat16)
    local_delta = local_delta.reshape(doc_count, owned_groups * splitting, slice_rows, columns)
    delta_blocks = local_delta
    grad_sum = jnp.einsum("kgptc,kptd->gcd", owned, grads, preferred_element_type=jnp.float32)
    grad_sum, delta_blocks = (grad_sum, delta_blocks)
    grad_out_proj = (
        lax.psum(grad_sum, "seq").reshape(width // dp_devices, model_width).astype(jnp.bfloat16)
    )
    delta_head = lax.all_to_all(
        lax.all_to_all(delta_blocks, "dp", split_axis=0, concat_axis=1, tiled=True),
        "seq",
        split_axis=1,
        concat_axis=1,
        tiled=True,
    )
    delta_blk = delta_head.reshape(query_blocks, BLOCK, heads_here, HEAD_DIM)
    prob_grad = jnp.concatenate(
        [
            jnp.einsum("bqhe,bkhe->bhqk", delta_blk, value_win, preferred_element_type=jnp.float32),
            jnp.einsum("bqhe,khe->bhqk", delta_blk, value_glob, preferred_element_type=jnp.float32),
        ],
        axis=-1,
    )
    keep_rows = (
        jnp.where(is_global, 0.0, 1.0).astype(jnp.float32).reshape(query_blocks, 1, BLOCK, 1)
    )
    score_bf = (
        prob_rows * (prob_grad - jnp.sum(prob_rows * prob_grad, axis=-1, keepdims=True)) * keep_rows
    ).astype(jnp.bfloat16)
    prob_kept = prob_bf * keep_rows.astype(jnp.bfloat16)
    grad_query = jnp.einsum(
        "bhqk,bkhe->bqhe", score_bf[..., :window_keys], key_win, preferred_element_type=jnp.float32
    )
    grad_query = (
        grad_query
        + jnp.einsum(
            "bhqk,khe->bqhe",
            score_bf[..., window_keys:],
            key_glob,
            preferred_element_type=jnp.float32,
        )
    ) * scaling
    flat_ids = block_ids.reshape(-1)
    key_part = (
        jnp.einsum(
            "bhqk,bqhe->bkhe",
            score_bf[..., :window_keys],
            query_blk,
            preferred_element_type=jnp.float32,
        )
        * scaling
    )
    key_globpart = (
        jnp.einsum(
            "bhqk,bqhe->khe",
            score_bf[..., window_keys:],
            query_blk,
            preferred_element_type=jnp.float32,
        )
        * scaling
    )
    value_part = jnp.einsum(
        "bhqk,bqhe->bkhe",
        prob_kept[..., :window_keys],
        delta_blk,
        preferred_element_type=jnp.float32,
    )
    value_globpart = jnp.einsum(
        "bhqk,bqhe->khe",
        prob_kept[..., window_keys:],
        delta_blk,
        preferred_element_type=jnp.float32,
    )
    grad_key = (
        jnp.zeros((block_total, BLOCK, columns), jnp.float32)
        .at[flat_ids]
        .add(key_part.reshape(-1, BLOCK, columns))
        .reshape(seq_length, columns)
    )
    grad_key = grad_key.at[doc_globals].add(key_globpart.reshape(global_count, columns))
    grad_value = (
        jnp.zeros((block_total, BLOCK, columns), jnp.float32)
        .at[flat_ids]
        .add(value_part.reshape(-1, BLOCK, columns))
        .reshape(seq_length, columns)
    )
    grad_value = grad_value.at[doc_globals].add(value_globpart.reshape(global_count, columns))
    delta_glob = (
        jnp.einsum(
            "ng,nc->gc",
            picker,
            delta_head.reshape(query_count, columns),
            preferred_element_type=jnp.float32,
        )
        .astype(jnp.bfloat16)
        .reshape(global_count, heads_here, HEAD_DIM)
    )
    prob_grad_glob = jnp.einsum(
        "ghe,the->hgt", delta_glob, value_all, preferred_element_type=jnp.float32
    )
    score_glob_bf = (
        prob_glob * (prob_grad_glob - jnp.sum(prob_glob * prob_grad_glob, axis=-1, keepdims=True))
    ).astype(jnp.bfloat16)
    grad_query_glob = (
        jnp.einsum(
            "hgt,the->ghe", score_glob_bf, key_all, preferred_element_type=jnp.float32
        ).reshape(global_count, columns)
        * scaling
    )
    grad_key = (
        grad_key
        + jnp.einsum(
            "hgt,ghe->the", score_glob_bf, query_glob, preferred_element_type=jnp.float32
        ).reshape(seq_length, columns)
        * scaling
    )
    grad_value = grad_value + jnp.einsum(
        "hgt,ghe->the", prob_glob_bf, delta_glob, preferred_element_type=jnp.float32
    ).reshape(seq_length, columns)
    grad_query_all = grad_query.reshape(query_count, columns) + jnp.dot(
        picker_f, grad_query_glob, precision=lax.Precision.HIGHEST
    )
    query_back, key_back, value_back = (
        lax.all_to_all(
            grad_query_all.reshape(seq_devices, slice_rows, columns),
            "seq",
            split_axis=0,
            concat_axis=0,
            tiled=True,
        ),
        lax.all_to_all(
            grad_key.reshape(seq_devices, tokens, columns),
            "seq",
            split_axis=0,
            concat_axis=0,
            tiled=True,
        ),
        lax.all_to_all(
            grad_value.reshape(seq_devices, tokens, columns),
            "seq",
            split_axis=0,
            concat_axis=0,
            tiled=True,
        ),
    )

    def fold_pairs(received):
        summed = jnp.sum(received.reshape(head_groups, splitting, tokens, columns), axis=1)
        return summed.transpose(1, 0, 2).reshape(1, tokens, width).astype(jnp.bfloat16)

    grad_queries = (
        query_back.reshape(head_groups, splitting, slice_rows, columns)
        .transpose(1, 2, 0, 3)
        .reshape(1, tokens, width)
        .astype(jnp.bfloat16)
    )
    grad_keys = fold_pairs(key_back)
    grad_values = fold_pairs(value_back)
    return (grad_queries, grad_keys, grad_values, grad_out_proj)


def solution(mesh):
    return jax.shard_map(
        shards,
        mesh=mesh,
        in_specs=(
            P("dp", "seq", None),
            P("dp", "seq", None),
            P("dp", "seq", None),
            P("dp", "seq", None),
            P("dp", None, None),
            P("dp", None),
            P("dp", None),
        ),
        out_specs=(P("dp", "seq", None), P("dp", "seq", None), P("dp", "seq", None), P("dp", None)),
        check_vma=False,
    )
```

profile of v0, /device:TPU:8, one launch (start us, length us, event | category | flops | bytes accessed | tf_op | source)
XLA Modules:
  0.0 553.9 jit_solution(5008034609323652215)
XLA Ops:
  10.0 11.3 %all-to-all-start.1 = ((bf16[32,64,128]{2,1,0:T(8,128)(2,1)}), bf16[32,64,128]{2,1,0:T(8,128)(2,1)S(1)}, u32[]{:S(2)}, u32[]{:S(2)}) async-start(bf16[32,64,128]{2,1,0:T(8,128)(2,1)} %bitcast.8), calls=%async_computation.1 | async-start | bytes 1048576 | tf_op jit(solution)/shard_map/all_to_all | solution.py:59
  21.7 17.5 %all-to-all-done.1 = bf16[32,64,128]{2,1,0:T(8,128)(2,1)S(1)} async-done(((bf16[32,64,128]{2,1,0:T(8,128)(2,1)}), bf16[32,64,128]{2,1,0:T(8,128)(2,1)S(1)}, u32[]{:S(2)}, u32[]{:S(2)}) %all-to-all-start.1) | async-done | bytes 524320 | tf_op jit(solution)/shard_map/all_to_all | solution.py:59
  40.3 4.6 all-to-all-start
  47.6 24.6 %all-to-all-done = bf16[32,128,128]{2,1,0:T(8,128)(2,1)S(1)} async-done(((bf16[32,128,128]{2,1,0:T(8,128)(2,1)}), bf16[32,128,128]{2,1,0:T(8,128)(2,1)S(1)}, u32[]{:S(2)}, u32[]{:S(2)}) %all-to-all-start) | async-done | bytes 1048608 | tf_op jit(solution)/shard_map/all_to_all | solution.py:60
  74.5 5.7 %all-to-all-start.4 = ((bf16[32,128,128]{2,1,0:T(8,128)(2,1)}), bf16[32,128,128]{2,1,0:T(8,128)(2,1)}, u32[]{:S(2)}, u32[]{:S(2)}) async-start(bf16[32,128,128]{2,1,0:T(8,128)(2,1)} %bitcast.285), calls=%async_computation.4 | async-start | bytes 2097152 | tf_op jit(solution)/shard_map/all_to_all | solution.py:61
  87.0 20.0 %all-to-all-done.4 = bf16[32,128,128]{2,1,0:T(8,128)(2,1)} async-done(((bf16[32,128,128]{2,1,0:T(8,128)(2,1)}), bf16[32,128,128]{2,1,0:T(8,128)(2,1)}, u32[]{:S(2)}, u32[]{:S(2)}) %all-to-all-start.4) | async-done | bytes 1048608 | tf_op jit(solution)/shard_map/all_to_all | solution.py:61
  130.7 5.7 %all-to-all-start.8 = ((bf16[1,32,64,128]{3,2,0,1:T(8,128)(2,1)}), bf16[1,32,64,128]{3,2,0,1:T(8,128)(2,1)}, u32[]{:S(2)}, u32[]{:S(2)}) async-start(bf16[1,32,64,128]{3,2,0,1:T(8,128)(2,1)} %bitcast.302), calls=%async_computation.8 | async-start | bytes 1048576 | tf_op jit(solution)/shard_map/all_to_all | solution.py:131
  136.4 4.9 fusion.24
  141.4 11.4 %all-to-all-done.8 = bf16[1,32,64,128]{3,2,0,1:T(8,128)(2,1)} async-done(((bf16[1,32,64,128]{3,2,0,1:T(8,128)(2,1)}), bf16[1,32,64,128]{3,2,0,1:T(8,128)(2,1)}, u32[]{:S(2)}, u32[]{:S(2)}) %all-to-all-start.8) | async-done | bytes 524320 | tf_op jit(solution)/shard_map/all_to_all | solution.py:131
  152.8 13.7 %all_to_all.61 = bf16[8,4,64,128]{3,2,1,0:T(8,128)(2,1)} all-to-all(bf16[8,4,64,128]{3,2,1,0:T(8,128)(2,1)S(1)} %bitcast.290), channel_id=1, replica_groups=mesh['seq'=32,'dp'=8] {'dp'}, dimensions={0} | all-to-all | bytes 1048576 | tf_op jit(solution)/shard_map/all_to_all | solution.py:159
  166.5 4.4 all-to-all-start.3
  171.1 17.2 %all-to-all-done.3 = bf16[1,32,64,128]{3,2,0,1:T(8,128)(2,1)S(1)} async-done(((bf16[1,32,64,128]{3,2,0,1:T(8,128)(2,1)}), bf16[1,32,64,128]{3,2,0,1:T(8,128)(2,1)S(1)}, u32[]{:S(2)}, u32[]{:S(2)}) %all-to-all-start.3) | async-done | bytes 524320 | tf_op jit(solution)/shard_map/all_to_all | solution.py:158
  188.3 5.5 all-to-all-start.9
  209.9 4.9 all-to-all-start.5
  214.9 5.1 convolution_bitcast_fusion.2
  220.0 6.5 %copy.128 = f32[32,384,1,128]{3,1,0,2:T(8,128)} copy(f32[32,384,1,128]{1,3,0,2:T(8,128)} %convolution_bitcast_fusion.2) | data formatting | bytes 12582912 | tf_op jit(solution)/shard_map/bhqk,bqhe->bkhe/transpose | solution.py:211
  226.8 20.0 %scatter_fusion.2 = f32[64,64,128]{2,1,0:T(8,128)S(1)} fusion(f32[64,64,128]{2,1,0:T(8,128)S(1)} %broadcast.440.clone.1, s32[192]{0:T(256)S(1)} %bitcast.304, f32[192,64,128]{2,1,0:T(8,128)} %bitcast.276), kind=kCustom, calls=%fused_computation.7 | custom fusion | flops 1572864 | bytes 18875136 | tf_op jit(solution)/shard_map/scatter-add | solution.py:233
  248.6 4.3 fusion
  260.5 9.8 %all-to-all-start.7 = ((f32[32,128,128]{2,1,0:T(8,128)}), f32[32,128,128]{2,1,0:T(8,128)}, u32[]{:S(2)}, u32[]{:S(2)}) async-start(f32[32,128,128]{2,1,0:T(8,128)} %bitcast.278), calls=%async_computation.7 | async-start | bytes 4194304 | tf_op jit(solution)/shard_map/all_to_all | solution.py:287
  274.3 20.0 %scatter_fusion = f32[64,64,128]{2,1,0:T(8,128)S(1)} fusion(f32[64,64,128]{2,1,0:T(8,128)S(1)} %broadcast.440.clone, s32[192]{0:T(256)S(1)} %bitcast.305, f32[192,64,128]{2,1,0:T(8,128)} %bitcast.277), kind=kCustom, calls=%fused_computation.5 | custom fusion | flops 1572864 | bytes 18875136 | tf_op jit(solution)/shard_map/scatter-add | solution.py:226
  307.9 12.3 %all-to-all-done.7 = f32[32,128,128]{2,1,0:T(8,128)} async-done(((f32[32,128,128]{2,1,0:T(8,128)}), f32[32,128,128]{2,1,0:T(8,128)}, u32[]{:S(2)}, u32[]{:S(2)}) %all-to-all-start.7) | async-done | bytes 2097184 | tf_op jit(solution)/shard_map/all_to_all | solution.py:287
  320.2 6.1 %all-to-all-start.6 = ((f32[32,128,128]{2,1,0:T(8,128)}), f32[32,128,128]{2,1,0:T(8,128)}, u32[]{:S(2)}, u32[]{:S(2)}) async-start(f32[32,128,128]{2,1,0:T(8,128)} %bitcast.68), calls=%async_computation.6 | async-start | bytes 4194304 | tf_op jit(solution)/shard_map/all_to_all | solution.py:280
  326.3 7.9 %convolution_bitcast_fusion = f32[2,128,4096]{2,1,0:T(8,128)} fusion(bf16[8,2,2,64,128]{4,3,2,1,0:T(8,128)(2,1)} %bitcast.98, bf16[8,2,64,4096,1]{3,2,1,4,0:T(8,128)(2,1)} %bitcast.281), kind=kOutput, calls=%fused_computation.9 | convolution fusion | flops 2147483648 | bytes 13107200 | tf_op jit(solution)/shard_map/kgptc,kptd->gcd/dot_general | solution.py:153
  334.2 205.3 %all-reduce.2 = bf16[2,128,4096]{2,1,0:T(8,128)(2,1)} all-reduce(f32[2,128,4096]{2,1,0:T(8,128)} %convolution_bitcast_fusion), channel_id=1, replica_groups=mesh['seq'=32,'dp'=8] {'seq'}, use_global_device_ids=true, to_apply=%region_14.16 | all-reduce | flops 1048576 | bytes 6291456 | tf_op jit(solution)/shard_map/psum | solution.py:156
  (148 shorter events, 90.6 us)
Async XLA Ops:
  7.2 129.3 %copy-start = (bf16[256,4096]{1,0:T(8,128)(2,1)S(1)}, bf16[256,4096]{1,0:T(8,128)(2,1)}, u32[]{:S(2)}) copy-start(bf16[256,4096]{1,0:T(8,128)(2,1)} %param.15) | copy-start | bytes 6291460
  7.2 14.2 %copy-start.23 = (bf16[1,128,2048]{2,1,0:T(8,128)(2,1)S(1)}, bf16[1,128,2048]{2,1,0:T(8,128)(2,1)}, u32[]{:S(2)}) copy-start(bf16[1,128,2048]{2,1,0:T(8,128)(2,1)} %param.10) | copy-start | bytes 1572868
  7.2 129.2 %all-gather.2.cloned.1.call-start = ((), (), s32[]{:S(2)}) async-start(), calls=%async_computation.10 | async-start | bytes 9437184 | tf_op jit(solution)/shard_map/all_gather | solution.py:145
  10.0 29.1 %all-to-all-start.1 = ((bf16[32,64,128]{2,1,0:T(8,128)(2,1)}), bf16[32,64,128]{2,1,0:T(8,128)(2,1)S(1)}, u32[]{:S(2)}, u32[]{:S(2)}) async-start(bf16[32,64,128]{2,1,0:T(8,128)(2,1)} %bitcast.8), calls=%async_computation.1 | async-start | bytes 1048576 | tf_op jit(solution)/shard_map/all_to_all | solution.py:59
  21.6 23.4 %copy-start.25 = (s32[1,64,3]{1,0,2:T(1,128)S(1)}, s32[1,64,3]{1,0,2:T(1,128)}, u32[]{:S(2)}) copy-start(s32[1,64,3]{1,0,2:T(1,128)} %param.13) | copy-start | bytes 2308
  40.3 31.8 %all-to-all-start = ((bf16[32,128,128]{2,1,0:T(8,128)(2,1)}), bf16[32,128,128]{2,1,0:T(8,128)(2,1)S(1)}, u32[]{:S(2)}, u32[]{:S(2)}) async-start(bf16[32,128,128]{2,1,0:T(8,128)(2,1)} %bitcast.284), calls=%async_computation | async-start | bytes 2097152 | tf_op jit(solution)/shard_map/all_to_all | solution.py:60
  47.4 34.2 %copy-start.24 = (s32[1,128]{1,0:T(1,128)S(1)}, s32[1,128]{1,0:T(1,128)}, u32[]{:S(2)}) copy-start(s32[1,128]{1,0:T(1,128)} %param.14) | copy-start | bytes 1540
  74.5 32.5 %all-to-all-start.4 = ((bf16[32,128,128]{2,1,0:T(8,128)(2,1)}), bf16[32,128,128]{2,1,0:T(8,128)(2,1)}, u32[]{:S(2)}, u32[]{:S(2)}) async-start(bf16[32,128,128]{2,1,0:T(8,128)(2,1)} %bitcast.285), calls=%async_computation.4 | async-start | bytes 2097152 | tf_op jit(solution)/shard_map/all_to_all | solution.py:61
  115.3 6.6 %copy-start.6 = (f32[32,1,64,128]{3,2,0,1:T(8,128)}, f32[32,1,64,128]{3,2,0,1:T(8,128)S(1)}, u32[]{:S(2)}) copy-start(f32[32,1,64,128]{3,2,0,1:T(8,128)S(1)} %get-tuple-element.28) | copy-start | bytes 3145732
  119.8 6.2 %copy-start.8 = (f32[128,4096]{1,0:T(8,128)}, f32[128,4096]{1,0:T(8,128)S(1)}, u32[]{:S(2)}) copy-start(f32[128,4096]{1,0:T(8,128)S(1)} %get-tuple-element.30) | copy-start | bytes 6291460
  130.7 22.1 %all-to-all-start.8 = ((bf16[1,32,64,128]{3,2,0,1:T(8,128)(2,1)}), bf16[1,32,64,128]{3,2,0,1:T(8,128)(2,1)}, u32[]{:S(2)}, u32[]{:S(2)}) async-start(bf16[1,32,64,128]{3,2,0,1:T(8,128)(2,1)} %bitcast.302), calls=%async_computation.8 | async-start | bytes 1048576 | tf_op jit(solution)/shard_map/all_to_all | solution.py:131
  166.5 21.8 %all-to-all-start.3 = ((bf16[1,32,64,128]{3,2,0,1:T(8,128)(2,1)}), bf16[1,32,64,128]{3,2,0,1:T(8,128)(2,1)S(1)}, u32[]{:S(2)}, u32[]{:S(2)}) async-start(bf16[1,32,64,128]{3,2,0,1:T(8,128)(2,1)} %bitcast.28), calls=%async_computation.3 | async-start | bytes 1048576 | tf_op jit(solution)/shard_map/all_to_all | solution.py:158
  188.3 9.8 %copy-start.18 = (bf16[1,32,64,128]{3,2,0,1:T(8,128)(2,1)}, bf16[1,32,64,128]{3,2,0,1:T(8,128)(2,1)S(1)}, u32[]{:S(2)}) copy-start(bf16[1,32,64,128]{3,2,0,1:T(8,128)(2,1)S(1)} %all-to-all-done.3) | copy-start | bytes 1572868
  188.3 21.6 %all-to-all-start.9 = ((bf16[1,32,64,128]{3,2,0,1:T(8,128)(2,1)}), bf16[1,32,64,128]{3,2,0,1:T(8,128)(2,1)}, u32[]{:S(2)}, u32[]{:S(2)}) async-start(bf16[1,32,64,128]{3,2,0,1:T(8,128)(2,1)} %all-to-all-done.8), calls=%async_computation.9 | async-start | bytes 1048576 | tf_op jit(solution)/shard_map/all_to_all | solution.py:130
  194.5 4.0 copy-start.3
  202.5 3.7 copy-start.10
  207.3 7.6 %copy-start.19 = (bf16[1,32,64,128]{3,2,0,1:T(8,128)(2,1)S(1)}, bf16[1,32,64,128]{3,2,0,1:T(8,128)(2,1)}, u32[]{:S(2)}) copy-start(bf16[1,32,64,128]{3,2,0,1:T(8,128)(2,1)} %copy-done.18) | copy-start | bytes 1572868
  209.9 48.4 %all-to-all-start.5 = ((bf16[32,64,128]{2,1,0:T(8,128)(2,1)}), bf16[32,64,128]{2,1,0:T(8,128)(2,1)S(1)}, u32[]{:S(2)}, u32[]{:S(2)}) async-start(bf16[32,64,128]{2,1,0:T(8,128)(2,1)} %bitcast.53), calls=%async_computation.5 | async-start | bytes 1048576 | tf_op jit(solution)/shard_map/all_to_all | solution.py:273
  259.7 10.6 %copy-start.11 = (bf16[32,1,64,512]{3,2,0,1:T(8,128)(2,1)S(1)}, bf16[32,1,64,512]{3,2,0,1:T(8,128)(2,1)}, u32[]{:S(2)}) copy-start(bf16[32,1,64,512]{3,2,0,1:T(8,128)(2,1)} %copy-done.10) | copy-start | bytes 6291460
  259.7 10.6 %copy-start.16 = (bf16[32,64,128]{2,1,0:T(8,128)(2,1)S(1)}, bf16[32,64,128]{2,1,0:T(8,128)(2,1)}, u32[]{:S(2)}) copy-start(bf16[32,64,128]{2,1,0:T(8,128)(2,1)} %copy-done.15) | copy-start | bytes 1572868
  260.5 59.7 %all-to-all-start.7 = ((f32[32,128,128]{2,1,0:T(8,128)}), f32[32,128,128]{2,1,0:T(8,128)}, u32[]{:S(2)}, u32[]{:S(2)}) async-start(f32[32,128,128]{2,1,0:T(8,128)} %bitcast.278), calls=%async_computation.7 | async-start | bytes 4194304 | tf_op jit(solution)/shard_map/all_to_all | solution.py:287
  320.2 223.8 %all-to-all-start.6 = ((f32[32,128,128]{2,1,0:T(8,128)}), f32[32,128,128]{2,1,0:T(8,128)}, u32[]{:S(2)}, u32[]{:S(2)}) async-start(f32[32,128,128]{2,1,0:T(8,128)} %bitcast.68), calls=%async_computation.6 | async-start | bytes 4194304 | tf_op jit(solution)/shard_map/all_to_all | solution.py:280
  334.2 205.3 %copy-start.22 = (bf16[32,64,128]{2,1,0:T(8,128)(2,1)S(1)}, bf16[32,64,128]{2,1,0:T(8,128)(2,1)}, u32[]{:S(2)}) copy-start(bf16[32,64,128]{2,1,0:T(8,128)(2,1)} %copy-done.21) | copy-start | bytes 1572868
  542.9 4.1 copy-start.1
  (12 other events, 21.1 us)
Sparse Core Ops, SparseCore 0:
  9.9 54.2 all-gather.1
where the time goes:
time: 557 us; the launch traced here: 554 us
  blocking collectives  219 us (39%)
  waiting for transfers between devices  104 us (19%)
  other arithmetic  59 us (11%)
  starting transfers between devices  58.1 us (10%)
  matrix products  56.2 us (10%)
  local copies, waits for them, and re-layouts  43.3 us (8%)
  between operations  14.7 us (3%)
    psum x1, blocking collectives, shards(): lax.psum(grad_sum, 'seq').reshape(width // dp_devices, model_width)  205 us
    all_to_all x1, waiting for transfers between devices, shards(): lax.all_to_all(spread(key_rows), 'seq', split_axis=0, concat_axis=0, tile...  24.6 us
    all_to_all x1, waiting for transfers between devices, shards(): lax.all_to_all(spread(value_rows), 'seq', split_axis=0, concat_axis=0, ti...  20 us
    scatter-add x1, other arithmetic, shards(): grad_value = jnp.zeros((block_total, BLOCK, columns), jnp.float32).at[fla...  20 us
    scatter-add x1, other arithmetic, shards(): grad_key = jnp.zeros((block_total, BLOCK, columns), jnp.float32).at[flat_...  20 us
    all_to_all x1, waiting for transfers between devices, shards(): lax.all_to_all(query_send, 'seq', split_axis=0, concat_axis=0, tiled=True)  17.5 us
    all_to_all x1, waiting for transfers between devices, shards(): lax.all_to_all(lax.all_to_all(delta_blocks, 'dp', split_axis=0, concat_ax...  17.2 us
    all_to_all x1, blocking collectives, shards(): lax.all_to_all(delta_blocks, 'dp', split_axis=0, concat_axis=1, tiled=True)  13.7 us
  transfers between devices with their start and end apart: 10, of which 6 were waited for; matrix products, arithmetic and copies ran while one was open for 27% of the time, Pallas kernels for 0%

commit v1 on v0

--- a/solution.py
+++ b/solution.py
@@ -152,9 +152,10 @@
     delta_blocks = local_delta
     grad_sum = jnp.einsum("kgptc,kptd->gcd", owned, grads, preferred_element_type=jnp.float32)
     grad_sum, delta_blocks = (grad_sum, delta_blocks)
-    grad_out_proj = (
-        lax.psum(grad_sum, "seq").reshape(width // dp_devices, model_width).astype(jnp.bfloat16)
-    )
+    grad_part = lax.psum_scatter(
+        grad_sum.reshape(width // dp_devices, model_width), "seq", scatter_dimension=0, tiled=True
+    )
+    grad_out_proj = lax.all_gather(grad_part.astype(jnp.bfloat16), "seq", axis=0, tiled=True)
     delta_head = lax.all_to_all(
         lax.all_to_all(delta_blocks, "dp", split_axis=0, concat_axis=1, tiled=True),
         "seq",
@@ -271,21 +272,21 @@
     )
     query_back, key_back, value_back = (
         lax.all_to_all(
-            grad_query_all.reshape(seq_devices, slice_rows, columns),
+            grad_query_all.astype(jnp.bfloat16).reshape(seq_devices, slice_rows, columns),
             "seq",
             split_axis=0,
             concat_axis=0,
             tiled=True,
         ),
         lax.all_to_all(
-            grad_key.reshape(seq_devices, tokens, columns),
+            grad_key.astype(jnp.bfloat16).reshape(seq_devices, tokens, columns),
             "seq",
             split_axis=0,
             concat_axis=0,
             tiled=True,
         ),
         lax.all_to_all(
-            grad_value.reshape(seq_devices, tokens, columns),
+            grad_value.astype(jnp.bfloat16).reshape(seq_devices, tokens, columns),
             "seq",
             split_axis=0,
             concat_axis=0,
@@ -294,7 +295,9 @@
     )
 
     def fold_pairs(received):
-        summed = jnp.sum(received.reshape(head_groups, splitting, tokens, columns), axis=1)
+        summed = jnp.sum(
+            received.astype(jnp.float32).reshape(head_groups, splitting, tokens, columns), axis=1
+        )
         return summed.transpose(1, 0, 2).reshape(1, tokens, width).astype(jnp.bfloat16)
 
     grad_queries = (

time: 557 us -> 495 us (0.89)
  blocking collectives: 219 us -> 49 us
  waiting for transfers between devices: 104 us -> 218 us
  starting transfers between devices: 58.1 us -> 47.6 us
    psum x1 -> x0, blocking collectives: 205 us -> none  [shards(): lax.psum(grad_sum, 'seq').reshape(width // dp_devices, model_width)]
    reduce_scatter x0 -> x1, waiting for transfers between devices: none -> 103 us  [shards(): lax.psum_scatter(grad_sum.reshape(width // dp_devices, model_width), 'seq...]
    all_to_all x0 -> x2, blocking collectives: none -> 35.4 us  [the longest x1 21.8 us: shards(): lax.all_to_all(attention.reshape(1, seq_devices, slice_rows, columns), 's...]
    all_to_all x5 -> x3, starting transfers between devices: 32 us -> 21.2 us  [the longest x1 9.69 us: shards(): lax.all_to_all(grad_value.astype(jnp.bfloat16).reshape(seq_devices, token...]
    all_gather x0 -> x1, waiting for transfers between devices: none -> 6.53 us  [shards(): lax.all_gather(grad_part.astype(jnp.bfloat16), 'seq', axis=0, tiled=True)]
    all_to_all x5 -> x3, waiting for transfers between devices: 23.8 us -> 25.6 us  [the longest x1 25.6 us: shards(): lax.all_to_all(grad_key.astype(jnp.bfloat16).reshape(seq_devices, tokens,...]
  transfers between devices with their start and end apart: 10 -> 10, of which waited for: 6 -> 7; matrix products, arithmetic and copies ran while one was open for 27% -> 30% of each run, Pallas kernels for 0% -> 0%
where the time goes in v1:
time: 495 us; the launch traced here: 492 us
  waiting for transfers between devices  218 us (44%)
  other arithmetic  62.5 us (13%)
  matrix products  54.2 us (11%)
  blocking collectives  49 us (10%)
  starting transfers between devices  47.6 us (10%)
  local copies, waits for them, and re-layouts  47.1 us (10%)
  between operations  14.4 us (3%)
    reduce_scatter x1, waiting for transfers between devices, shards(): lax.psum_scatter(grad_sum.reshape(width // dp_devices, model_width), 'seq...  103 us
    all_to_all x1, waiting for transfers between devices, shards(): lax.all_to_all(grad_key.astype(jnp.bfloat16).reshape(seq_devices, tokens,...  25.6 us
    all_to_all x1, waiting for transfers between devices, shards(): lax.all_to_all(spread(key_rows), 'seq', split_axis=0, concat_axis=0, tile...  24.6 us
    all_to_all x1, blocking collectives, shards(): lax.all_to_all(attention.reshape(1, seq_devices, slice_rows, columns), 's...  21.8 us
    scatter-add x1, other arithmetic, shards(): grad_value = jnp.zeros((block_total, BLOCK, columns), jnp.float32).at[fla...  20 us
    scatter-add x1, other arithmetic, shards(): grad_key = jnp.zeros((block_total, BLOCK, columns), jnp.float32).at[flat_...  20 us
    all_to_all x1, waiting for transfers between devices, shards(): lax.all_to_all(spread(value_rows), 'seq', split_axis=0, concat_axis=0, ti...  19.9 us
    all_to_all x1, waiting for transfers between devices, shards(): lax.all_to_all(lax.all_to_all(delta_blocks, 'dp', split_axis=0, concat_ax...  19.8 us
  transfers between devices with their start and end apart: 10, of which 7 were waited for; matrix products, arithmetic and copies ran while one was open for 30% of the time, Pallas kernels for 0%

profile of v1, /device:TPU:8, one launch (start us, length us, event | category | flops | bytes accessed | tf_op | source)
XLA Modules:
  0.0 492.4 jit_solution(7822460180789586121)
XLA Ops:
  10.0 11.3 %all-to-all-start.1 = ((bf16[32,64,128]{2,1,0:T(8,128)(2,1)}), bf16[32,64,128]{2,1,0:T(8,128)(2,1)S(1)}, u32[]{:S(2)}, u32[]{:S(2)}) async-start(bf16[32,64,128]{2,1,0:T(8,128)(2,1)} %bitcast.8), calls=%async_computation.1 | async-start | bytes 1048576 | tf_op jit(solution)/shard_map/all_to_all | solution.py:59
  21.7 17.5 %all-to-all-done.1 = bf16[32,64,128]{2,1,0:T(8,128)(2,1)S(1)} async-done(((bf16[32,64,128]{2,1,0:T(8,128)(2,1)}), bf16[32,64,128]{2,1,0:T(8,128)(2,1)S(1)}, u32[]{:S(2)}, u32[]{:S(2)}) %all-to-all-start.1) | async-done | bytes 524320 | tf_op jit(solution)/shard_map/all_to_all | solution.py:59
  40.4 4.6 all-to-all-start
  47.7 24.6 %all-to-all-done = bf16[32,128,128]{2,1,0:T(8,128)(2,1)S(1)} async-done(((bf16[32,128,128]{2,1,0:T(8,128)(2,1)}), bf16[32,128,128]{2,1,0:T(8,128)(2,1)S(1)}, u32[]{:S(2)}, u32[]{:S(2)}) %all-to-all-start) | async-done | bytes 1048608 | tf_op jit(solution)/shard_map/all_to_all | solution.py:60
  74.6 5.7 %all-to-all-start.4 = ((bf16[32,128,128]{2,1,0:T(8,128)(2,1)}), bf16[32,128,128]{2,1,0:T(8,128)(2,1)}, u32[]{:S(2)}, u32[]{:S(2)}) async-start(bf16[32,128,128]{2,1,0:T(8,128)(2,1)} %bitcast.282), calls=%async_computation.4 | async-start | bytes 2097152 | tf_op jit(solution)/shard_map/all_to_all | solution.py:61
  87.1 19.9 %all-to-all-done.4 = bf16[32,128,128]{2,1,0:T(8,128)(2,1)} async-done(((bf16[32,128,128]{2,1,0:T(8,128)(2,1)}), bf16[32,128,128]{2,1,0:T(8,128)(2,1)}, u32[]{:S(2)}, u32[]{:S(2)}) %all-to-all-start.4) | async-done | bytes 1048608 | tf_op jit(solution)/shard_map/all_to_all | solution.py:61
  130.1 21.8 %all_to_all.61 = bf16[1,32,64,128]{3,2,0,1:T(8,128)(2,1)S(1)} all-to-all(bf16[1,32,64,128]{3,2,0,1:T(8,128)(2,1)S(1)} %bitcast.302), channel_id=1, replica_groups=mesh['seq'=32,'dp'=8] {'seq'}, dimensions={1} | all-to-all | bytes 1048576 | tf_op jit(solution)/shard_map/all_to_all | solution.py:131
  151.9 13.6 %all_to_all.62 = bf16[1,32,64,128]{3,2,0,1:T(8,128)(2,1)S(1)} all-to-all(bf16[1,32,64,128]{3,2,0,1:T(8,128)(2,1)S(1)} %all_to_all.61), channel_id=1, replica_groups=mesh['seq'=32,'dp'=8] {'dp'}, dimensions={1} | all-to-all | bytes 1048576 | tf_op jit(solution)/shard_map/all_to_all | solution.py:130
  169.0 7.9 %convolution_bitcast_fusion = f32[256,4096]{1,0:T(8,128)} fusion(bf16[256,8,2,64]{0,3,2,1:T(8,128)(2,1)} %dot_general.124, bf16[8,2,64,4096]{3,2,1,0:T(8,128)(2,1)} %bitcast.277), kind=kOutput, calls=%fused_computation.9 | convolution fusion | flops 2147483648 | bytes 13107200 | tf_op jit(solution)/shard_map/kgptc,kptd->gcd/dot_general | solution.py:153
  176.9 4.9 fusion.25
  181.9 13.6 %all_to_all.63 = bf16[8,4,64,128]{3,2,1,0:T(8,128)(2,1)} all-to-all(bf16[8,4,64,128]{3,2,1,0:T(8,128)(2,1)S(1)} %bitcast.290), channel_id=1, replica_groups=mesh['seq'=32,'dp'=8] {'dp'}, dimensions={0} | all-to-all | bytes 1048576 | tf_op jit(solution)/shard_map/all_to_all | solution.py:160
  195.4 4.6 all-to-all-start.3
  200.3 19.8 %all-to-all-done.3 = bf16[1,32,64,128]{3,2,0,1:T(8,128)(2,1)} async-done(((bf16[1,32,64,128]{3,2,0,1:T(8,128)(2,1)}), bf16[1,32,64,128]{3,2,0,1:T(8,128)(2,1)}, u32[]{:S(2)}, u32[]{:S(2)}) %all-to-all-start.3) | async-done | bytes 524320 | tf_op jit(solution)/shard_map/all_to_all | solution.py:159
  237.0 4.8 all-to-all-start.5
  241.8 4.7 convolution_bitcast_fusion.2
  246.5 6.6 %copy.133 = f32[32,384,1,128]{3,1,0,2:T(8,128)} copy(f32[32,384,1,128]{1,3,0,2:T(8,128)} %convolution_bitcast_fusion.2) | data formatting | bytes 12582912 | tf_op jit(solution)/shard_map/bhqk,bqhe->bkhe/transpose | solution.py:212
  253.3 20.0 %scatter_fusion.2 = f32[64,64,128]{2,1,0:T(8,128)S(1)} fusion(f32[64,64,128]{2,1,0:T(8,128)S(1)} %broadcast.440.clone.1, s32[192]{0:T(256)S(1)} %bitcast.304, f32[192,64,128]{2,1,0:T(8,128)} %bitcast.274), kind=kCustom, calls=%fused_computation.7 | custom fusion | flops 1572864 | bytes 18875136 | tf_op jit(solution)/shard_map/scatter-add | solution.py:234
  281.5 4.1 scatter_fusion.3
  288.4 9.7 %all-to-all-start.7 = ((bf16[32,128,128]{2,1,0:T(8,128)(2,1)}), bf16[32,128,128]{2,1,0:T(8,128)(2,1)}, u32[]{:S(2)}, u32[]{:S(2)}) async-start(bf16[32,128,128]{2,1,0:T(8,128)(2,1)} %bitcast.279), calls=%async_computation.7 | async-start | bytes 2097152 | tf_op jit(solution)/shard_map/all_to_all | solution.py:288
  298.1 103.0 %reduce-scatter.2.cloned.1.call-done = f32[8,4096]{1,0:T(8,128)} async-done(((f32[256,4096]{1,0:T(8,128)}), f32[8,4096]{1,0:T(8,128)}) %reduce-scatter.2.cloned.1.call-update) | async-done | bytes 131088 | tf_op jit(solution)/shard_map/reduce_scatter | solution.py:155
  406.6 20.0 %scatter_fusion = f32[64,64,128]{2,1,0:T(8,128)S(1)} fusion(f32[64,64,128]{2,1,0:T(8,128)S(1)} %broadcast.440.clone, s32[192]{0:T(256)S(1)} %bitcast.305, f32[192,64,128]{2,1,0:T(8,128)} %bitcast.275), kind=kCustom, calls=%fused_computation.5 | custom fusion | flops 1572864 | bytes 18875136 | tf_op jit(solution)/shard_map/scatter-add | solution.py:227
  438.3 6.7 %all-to-all-start.6 = ((bf16[32,128,128]{2,1,0:T(8,128)(2,1)}), bf16[32,128,128]{2,1,0:T(8,128)(2,1)S(1)}, u32[]{:S(2)}, u32[]{:S(2)}) async-start(bf16[32,128,128]{2,1,0:T(8,128)(2,1)} %bitcast.68), calls=%async_computation.6 | async-start | bytes 2097152 | tf_op jit(solution)/shard_map/all_to_all | solution.py:281
  449.1 25.6 %all-to-all-done.6 = bf16[32,128,128]{2,1,0:T(8,128)(2,1)S(1)} async-done(((bf16[32,128,128]{2,1,0:T(8,128)(2,1)}), bf16[32,128,128]{2,1,0:T(8,128)(2,1)S(1)}, u32[]{:S(2)}, u32[]{:S(2)}) %all-to-all-start.6) | async-done | bytes 1048608 | tf_op jit(solution)/shard_map/all_to_all | solution.py:281
  476.2 6.5 %all-gather.5.cloned.1.call-done = bf16[256,4096]{1,0:T(8,128)(2,1)} async-done(((bf16[8,4096]{1,0:T(8,128)(2,1)}), bf16[256,4096]{1,0:T(8,128)(2,1)}) %all-gather.5.cloned.1.call-update) | async-done | bytes 2097168 | tf_op jit(solution)/shard_map/all_gather | solution.py:158
  (153 shorter events, 96.6 us)
Async XLA Ops:
  7.2 169.8 %copy-start = (bf16[256,4096]{1,0:T(8,128)(2,1)S(1)}, bf16[256,4096]{1,0:T(8,128)(2,1)}, u32[]{:S(2)}) copy-start(bf16[256,4096]{1,0:T(8,128)(2,1)} %param.15) | copy-start | bytes 6291460
  7.2 14.2 %copy-start.21 = (bf16[1,128,2048]{2,1,0:T(8,128)(2,1)S(1)}, bf16[1,128,2048]{2,1,0:T(8,128)(2,1)}, u32[]{:S(2)}) copy-start(bf16[1,128,2048]{2,1,0:T(8,128)(2,1)} %param.10) | copy-start | bytes 1572868
  7.2 161.8 %all-gather.3.cloned.1.call-start = ((), (), s32[]{:S(2)}) async-start(), calls=%async_computation.11 | async-start | bytes 9437184 | tf_op jit(solution)/shard_map/all_gather | solution.py:145
  10.0 29.1 %all-to-all-start.1 = ((bf16[32,64,128]{2,1,0:T(8,128)(2,1)}), bf16[32,64,128]{2,1,0:T(8,128)(2,1)S(1)}, u32[]{:S(2)}, u32[]{:S(2)}) async-start(bf16[32,64,128]{2,1,0:T(8,128)(2,1)} %bitcast.8), calls=%async_computation.1 | async-start | bytes 1048576 | tf_op jit(solution)/shard_map/all_to_all | solution.py:59
  21.6 23.4 %copy-start.23 = (s32[1,64,3]{1,0,2:T(1,128)S(1)}, s32[1,64,3]{1,0,2:T(1,128)}, u32[]{:S(2)}) copy-start(s32[1,64,3]{1,0,2:T(1,128)} %param.13) | copy-start | bytes 2308
  40.4 31.8 %all-to-all-start = ((bf16[32,128,128]{2,1,0:T(8,128)(2,1)}), bf16[32,128,128]{2,1,0:T(8,128)(2,1)S(1)}, u32[]{:S(2)}, u32[]{:S(2)}) async-start(bf16[32,128,128]{2,1,0:T(8,128)(2,1)} %bitcast.281), calls=%async_computation | async-start | bytes 2097152 | tf_op jit(solution)/shard_map/all_to_all | solution.py:60
  47.4 34.2 %copy-start.22 = (s32[1,128]{1,0:T(1,128)S(1)}, s32[1,128]{1,0:T(1,128)}, u32[]{:S(2)}) copy-start(s32[1,128]{1,0:T(1,128)} %param.14) | copy-start | bytes 1540
  74.6 32.5 %all-to-all-start.4 = ((bf16[32,128,128]{2,1,0:T(8,128)(2,1)}), bf16[32,128,128]{2,1,0:T(8,128)(2,1)}, u32[]{:S(2)}, u32[]{:S(2)}) async-start(bf16[32,128,128]{2,1,0:T(8,128)(2,1)} %bitcast.282), calls=%async_computation.4 | async-start | bytes 2097152 | tf_op jit(solution)/shard_map/all_to_all | solution.py:61
  80.3 320.8 %reduce-scatter.2.cloned.1.call-start = ((), (), s32[]{:S(2)}) async-start(), calls=%async_computation.12 | async-start | bytes 4325376 | tf_op jit(solution)/shard_map/reduce_scatter | solution.py:155
  115.3 6.6 %copy-start.7 = (f32[32,1,64,128]{3,2,0,1:T(8,128)}, f32[32,1,64,128]{3,2,0,1:T(8,128)S(1)}, u32[]{:S(2)}) copy-start(f32[32,1,64,128]{3,2,0,1:T(8,128)S(1)} %get-tuple-element.28) | copy-start | bytes 3145732
  119.8 6.3 %copy-start.9 = (f32[128,4096]{1,0:T(8,128)}, f32[128,4096]{1,0:T(8,128)S(1)}, u32[]{:S(2)}) copy-start(f32[128,4096]{1,0:T(8,128)S(1)} %get-tuple-element.30) | copy-start | bytes 6291460
  181.9 41.4 %copy-start.10 = (f32[128,4096]{1,0:T(8,128)S(1)}, f32[128,4096]{1,0:T(8,128)}, u32[]{:S(2)}) copy-start(f32[128,4096]{1,0:T(8,128)} %copy-done.9) | copy-start | bytes 6291460
  195.4 24.6 %all-to-all-start.3 = ((bf16[1,32,64,128]{3,2,0,1:T(8,128)(2,1)}), bf16[1,32,64,128]{3,2,0,1:T(8,128)(2,1)}, u32[]{:S(2)}, u32[]{:S(2)}) async-start(bf16[1,32,64,128]{3,2,0,1:T(8,128)(2,1)} %bitcast.287), calls=%async_computation.3 | async-start | bytes 1048576 | tf_op jit(solution)/shard_map/all_to_all | solution.py:159
  227.5 2.7 copy-start.8
  235.0 6.8 %copy-start.18 = (bf16[32,1,64,512]{3,2,0,1:T(8,128)(2,1)S(1)}, bf16[32,1,64,512]{3,2,0,1:T(8,128)(2,1)}, u32[]{:S(2)}) copy-start(bf16[32,1,64,512]{3,2,0,1:T(8,128)(2,1)} %get-tuple-element.19) | copy-start | bytes 6291460
  237.0 51.4 %all-to-all-start.5 = ((bf16[32,64,128]{2,1,0:T(8,128)(2,1)}), bf16[32,64,128]{2,1,0:T(8,128)(2,1)S(1)}, u32[]{:S(2)}, u32[]{:S(2)}) async-start(bf16[32,64,128]{2,1,0:T(8,128)(2,1)} %bitcast.286), calls=%async_computation.5 | async-start | bytes 1048576 | tf_op jit(solution)/shard_map/all_to_all | solution.py:274
  285.6 117.1 %copy-start.12 = (bf16[32,1,64,512]{3,2,0,1:T(8,128)(2,1)S(1)}, bf16[32,1,64,512]{3,2,0,1:T(8,128)(2,1)}, u32[]{:S(2)}) copy-start(bf16[32,1,64,512]{3,2,0,1:T(8,128)(2,1)} %copy-done.11) | copy-start | bytes 6291460
  285.6 117.1 %copy-start.16 = (bf16[32,64,128]{2,1,0:T(8,128)(2,1)S(1)}, bf16[32,64,128]{2,1,0:T(8,128)(2,1)}, u32[]{:S(2)}) copy-start(bf16[32,64,128]{2,1,0:T(8,128)(2,1)} %copy-done.15) | copy-start | bytes 1572868
  288.4 118.0 %copy-start.19 = (bf16[32,64,128]{2,1,0:T(8,128)(2,1)}, bf16[32,64,128]{2,1,0:T(8,128)(2,1)S(1)}, u32[]{:S(2)}) copy-start(bf16[32,64,128]{2,1,0:T(8,128)(2,1)S(1)} %all-to-all-done.5) | copy-start | bytes 1572868
  288.4 149.9 %all-to-all-start.7 = ((bf16[32,128,128]{2,1,0:T(8,128)(2,1)}), bf16[32,128,128]{2,1,0:T(8,128)(2,1)}, u32[]{:S(2)}, u32[]{:S(2)}) async-start(bf16[32,128,128]{2,1,0:T(8,128)(2,1)} %bitcast.279), calls=%async_computation.7 | async-start | bytes 2097152 | tf_op jit(solution)/shard_map/all_to_all | solution.py:288
  298.1 184.6 %all-gather.5.cloned.1.call-start = ((), (), s32[]{:S(2)}) async-start(), calls=%async_computation.13 | async-start | bytes 2162688 | tf_op jit(solution)/shard_map/all_gather | solution.py:158
  437.2 7.8 %copy-start.20 = (bf16[32,64,128]{2,1,0:T(8,128)(2,1)S(1)}, bf16[32,64,128]{2,1,0:T(8,128)(2,1)}, u32[]{:S(2)}) copy-start(bf16[32,64,128]{2,1,0:T(8,128)(2,1)} %copy-done.19) | copy-start | bytes 1572868
  438.3 36.4 %all-to-all-start.6 = ((bf16[32,128,128]{2,1,0:T(8,128)(2,1)}), bf16[32,128,128]{2,1,0:T(8,128)(2,1)S(1)}, u32[]{:S(2)}, u32[]{:S(2)}) async-start(bf16[32,128,128]{2,1,0:T(8,128)(2,1)} %bitcast.68), calls=%async_computation.6 | async-start | bytes 2097152 | tf_op jit(solution)/shard_map/all_to_all | solution.py:281
  475.1 10.7 %copy-start.1 = (bf16[256,4096]{1,0:T(8,128)(2,1)S(1)}, bf16[256,4096]{1,0:T(8,128)(2,1)}, u32[]{:S(2)}) copy-start(bf16[256,4096]{1,0:T(8,128)(2,1)} %param.15) | copy-start | bytes 6291460
  (10 other events, 18.6 us)
Sparse Core Ops, SparseCore 0:
  9.9 54.2 all-gather.2
  177.0 224.0 reduce-scatter.1
  403.7 78.9 all-gather.4
